TPU v7x, 512 devices: a whole 4x4x16 slice. The times are simulated.
512 devices in a mesh: gx: 32 (over z_hi, x, core), gy: 16 (over y, z_lo).
Axes of the slice: x: 4, y: 4, z: 16 (z_hi: 4, z_lo: 4; z = z_hi * 4 + z_lo), core: 2. Of those that a mesh axis runs over, the one named last changes fastest.
Arguments:
- orbitals: float32 [32, 64, 128, 512], P(None, 'gx', 'gy'), may hold values from -60 to 60
- potential: float32 [64, 128, 512], P('gx', 'gy'), may hold values from 0.2 to 2
- sign_bits: int32 [64, 128, 512], P('gx', 'gy'), may hold values from 0 to 1
- sampled_rows: int32 [32, 16, 8192], P('gx', 'gy'), may hold values from 0 to 8191, each once within a row
Outputs:
- rotated: float32 [32, 64, 128, 512], P(None, 'gx', 'gy')
- sketches: float32 [2, 32, 4096], P(None, None, ('gx', 'gy'))
- projected: float32 [32, 32], replicated
Inputs may be any that keep to these rules, and one draw needn't show every extreme that they name: Each block's row of sampled_rows holds every one of its 8192 cell numbers once.
All inputs are finite; a program needn't handle non-finite values.
Results may differ from a plain program's by a relative error of at most 0.00026.
Values sent between devices are 32-bit elements; how exact they have to be, the bound alone decides.
No kernel may reach another device: no remote copies, remote signals or barrier semaphores. Data moves between devices by JAX's collectives and lax.ppermute only.
A program may use at most 64 MiB of HBM per device.

v0:
```python
import jax
import jax.numpy as jnp
from jax import lax
from jax.sharding import PartitionSpec as P

M = 4096
HIGHEST = lax.Precision.HIGHEST
filter_center = 6.25
filter_half = 4.25


def padded_2(array, sides, width):
    for axis, dim in sides:
        size, length = (lax.axis_size(axis), array.shape[dim])
        up = [(i, (i + 1) % size) for i in range(size - 1)]
        down = [(j, i) for i, j in up]
        last = lax.slice_in_dim(array, length - width, length, axis=dim)
        initial = lax.slice_in_dim(array, 0, width, axis=dim)
        before = lax.ppermute(last, axis, up)
        after = lax.ppermute(initial, axis, down)
        array = jnp.concatenate([before, array, after], axis=dim)
    return array


def hadamard_table(order):
    index = jnp.arange(order, dtype=jnp.int32)
    parity = jnp.zeros((order, order), jnp.int32)
    for bit in range(order.bit_length() - 1):
        weight = 2**bit
        parity = parity + index[:, None] // weight % 2 * (index[None, :] // weight % 2)
    return (1 - 2 * (parity % 2)).astype(jnp.float32)


def second_diff(padded, axis, count):
    parts = [lax.slice_in_dim(padded, k, k + count, axis=axis) for k in range(5)]
    return (16.0 * (parts[1] + parts[3]) - (parts[0] + parts[4]) - 30.0 * parts[2]) / 12.0


def apply_ham(field, potential):
    padded = padded_2(field, (("gx", 1), ("gy", 2)), 2)
    x_padded = padded[:, :, 2:-2, :]
    y_padded = padded[:, 2:-2, :, :]
    z_padded = jnp.pad(field, ((0, 0), (0, 0), (0, 0), (2, 2)))
    total = second_diff(x_padded, 1, field.shape[1])
    total = total + second_diff(y_padded, 2, field.shape[2])
    total = total + second_diff(z_padded, 3, field.shape[3])
    return -0.5 * total + potential[None] * field


def shards(orbitals, potential, sign_bits, sampled_rows):
    first = (apply_ham(orbitals, potential) - filter_center * orbitals) / filter_half
    second = 2.0 * (apply_ham(first, potential) - filter_center * first) / filter_half - orbitals
    filtered = 2.0 * (apply_ham(second, potential) - filter_center * second) / filter_half - first
    applied = apply_ham(filtered, potential)
    count = orbitals.shape[0]
    cells = orbitals.shape[1] * orbitals.shape[2] * orbitals.shape[3]
    stacked = jnp.concatenate([filtered, applied], axis=0)
    sign_block = (2 * sign_bits - 1).astype(jnp.float32)
    flat = (stacked * sign_block[None]).reshape(2 * count, -1, 128)
    mixed = jnp.einsum("nac,cd->nad", flat, hadamard_table(128), precision=HIGHEST)
    mixed = jnp.einsum("ba,nac->nbc", hadamard_table(cells // 128), mixed, precision=HIGHEST)
    mixed = mixed.reshape(2 * count, cells)
    picked = jnp.take(mixed, sampled_rows[0, 0, :M], axis=1)
    devices = lax.axis_size("gx") * lax.axis_size("gy")
    term = (picked / jnp.sqrt(jnp.float32(M * devices))).reshape(2, count, M)
    width = M // devices
    total = lax.psum(term, ("gx", "gy"))
    position = lax.axis_index("gx") * lax.axis_size("gy") + lax.axis_index("gy")
    share = lax.dynamic_slice_in_dim(total, position * width, width, 2)
    gram = jnp.dot(total[0], total[0].T, precision=HIGHEST) / cells
    cross = jnp.dot(total[0], total[1].T, precision=HIGHEST) / cells
    lower = jnp.linalg.cholesky(gram)
    inverse = lax.linalg.triangular_solve(
        lower, jnp.eye(count, dtype=jnp.float32), left_side=True, lower=True
    )
    rotated = jnp.dot(inverse, filtered.reshape(count, -1), precision=HIGHEST).reshape(
        filtered.shape
    )
    inner = jnp.dot(jnp.dot(inverse, cross, precision=HIGHEST), inverse.T, precision=HIGHEST)
    projected = 0.5 * (inner + inner.T)
    return (rotated, share, projected)


def solution(mesh):
    in_specs = (
        P(None, "gx", "gy", None),
        P("gx", "gy", None),
        P("gx", "gy", None),
        P("gx", "gy", None),
    )
    out_specs = (P(None, "gx", "gy", None), P(None, None, ("gx", "gy")), P())
    return jax.shard_map(shards, mesh=mesh, in_specs=in_specs, out_specs=out_specs, check_vma=False)
```

profile of v0, /device:TPU:1, one launch (start us, length us, event | category | flops | bytes accessed | tf_op | source)
XLA Modules:
  0.0 938.2 jit_solution(11268816920238034277)
XLA Ops:
  7.2 1.9 copy.36
  9.1 4.5 collective-permute-start
  13.7 5.6 collective-permute-start.1
  19.3 6.1 collective-permute-done
  25.5 0.6 constant_dynamic-update-slice_fusion.1
  26.1 4.0 collective-permute-done.1
  30.2 0.1 fusion.159
  30.3 3.6 collective-permute-start.2
  33.9 1.3 collective-permute-start.3
  35.2 7.6 collective-permute-done.2
  42.8 28.2 %collective-permute-done.3 = f32[32,6,2,512]{3,0,2,1:T(8,128)S(1)} collective-permute-done((f32[32,6,2,512]{3,0,2,1:T(8,128)S(1)}, f32[32,6,2,512]{3,0,2,1:T(8,128)S(1)}, u32[]{:S(2)}, u32[]{:S(2)}) %collective-permute-start.3) | collective-permute-done | bytes 786464 | tf_op jit(solution)/shard_map/ppermute | solution.py:20
  71.0 1.6 broadcast_multiply_fusion
  72.6 2.7 collective-permute-start.4
  75.3 1.9 collective-permute-start.5
  77.3 9.8 %collective-permute-done.4 = f32[32,2,8,512]{3,0,2,1:T(8,128)S(1)} collective-permute-done((f32[32,2,8,512]{3,0,2,1:T(8,128)S(1)}, f32[32,2,8,512]{3,0,2,1:T(8,128)S(1)}, u32[]{:S(2)}, u32[]{:S(2)}) %collective-permute-start.4) | collective-permute-done | bytes 1048608 | tf_op jit(solution)/shard_map/ppermute | solution.py:19
  87.1 4.4 collective-permute-done.5
  91.6 7.8 collective-permute-start.6
  99.4 1.3 collective-permute-start.7
  100.7 7.6 collective-permute-done.6
  108.2 26.3 %collective-permute-done.7 = f32[32,6,2,512]{3,0,2,1:T(8,128)S(1)} collective-permute-done((f32[32,6,2,512]{3,0,2,1:T(8,128)S(1)}, f32[32,6,2,512]{3,0,2,1:T(8,128)S(1)}, u32[]{:S(2)}, u32[]{:S(2)}) %collective-permute-start.7) | collective-permute-done | bytes 786464 | tf_op jit(solution)/shard_map/ppermute | solution.py:20
  134.6 2.4 fusion.21
  136.9 1.9 collective-permute-start.8
  138.9 2.5 collective-permute-start.9
  141.3 9.2 collective-permute-done.8
  150.6 4.4 collective-permute-done.9
  155.1 3.0 collective-permute-start.10
  158.2 1.3 collective-permute-start.11
  159.5 7.5 collective-permute-done.10
  167.0 24.4 %collective-permute-done.11 = f32[32,6,2,512]{3,0,2,1:T(8,128)S(1)} collective-permute-done((f32[32,6,2,512]{3,0,2,1:T(8,128)S(1)}, f32[32,6,2,512]{3,0,2,1:T(8,128)S(1)}, u32[]{:S(2)}, u32[]{:S(2)}) %collective-permute-start.11) | collective-permute-done | bytes 786464 | tf_op jit(solution)/shard_map/ppermute | solution.py:20
  191.4 1.8 fusion.32
  193.2 1.9 collective-permute-start.12
  195.1 2.5 collective-permute-start.13
  197.7 9.1 collective-permute-done.12
  206.8 22.0 %collective-permute-done.13 = f32[32,2,8,512]{3,0,2,1:T(8,128)S(1)} collective-permute-done((f32[32,2,8,512]{3,0,2,1:T(8,128)S(1)}, f32[32,2,8,512]{3,0,2,1:T(8,128)S(1)}, u32[]{:S(2)}, u32[]{:S(2)}) %collective-permute-start.13) | collective-permute-done | bytes 1048608 | tf_op jit(solution)/shard_map/ppermute | solution.py:20
  228.8 1.5 pad_maximum_fusion.30
  230.3 3.5 collective-permute-start.14
  233.7 1.3 collective-permute-start.15
  235.1 0.6 copy.46
  235.7 6.3 collective-permute-done.14
  242.1 27.8 %collective-permute-done.15 = f32[32,6,2,512]{3,0,2,1:T(8,128)} collective-permute-done((f32[32,6,2,512]{3,0,2,1:T(8,128)}, f32[32,6,2,512]{3,0,2,1:T(8,128)}, u32[]{:S(2)}, u32[]{:S(2)}) %collective-permute-start.15) | collective-permute-done | bytes 786464 | tf_op jit(solution)/shard_map/ppermute | solution.py:20
  269.9 3.4 fusion.40
  273.2 1.6 copy.47
  274.8 1.3 concatenate.101
  276.1 2.0 fusion
  278.1 2.1 convolution_bitcast_fusion
  280.2 2.7 copy.57
  282.9 13.0 %gather_fusion = f32[4096,64]{1,0:T(8,128)S(1)} fusion(f32[64,8192]{0,1:T(8,128)} %bitcast.60, s32[4096]{0:T(1024)S(1)} %broadcast_clamp_fusion), kind=kCustom, calls=%fused_computation | custom fusion | bytes 2113536 | tf_op jit(solution)/shard_map/jit(_take)/gather | solution.py:63
  295.9 1.6 copy.49
  297.5 2.3 select_multiply_fusion
  299.8 0.6 copy.59
  300.4 614.8 %all-reduce.6.cloned.1.call-done = f32[2,32,4096]{2,1,0:T(8,128)} async-done(((f32[2,32,4096]{2,1,0:T(8,128)}), f32[2,32,4096]{2,1,0:T(8,128)}) %all-reduce.6.cloned.1.call-update) | async-done | bytes 1048592 | tf_op jit(solution)/shard_map/psum | solution.py:67
  915.2 1.8 fusion.81
  917.0 2.9 cholesky.17
  920.0 0.6 compare_reduce_fusion
  920.6 0.7 fusion.117
  921.3 2.4 custom-call.6
  923.7 0.2 fusion.120
  923.9 1.8 convolution_multiply_fusion
  925.9 0.2 fusion.161
  926.1 0.6 fusion.119
  926.7 1.6 fusion.78
  928.3 1.6 copy.54
  929.9 0.8 constant_dynamic-slice_fusion
  930.7 0.7 copy.55
  (39 shorter events, 1.0 us)
Async XLA Ops:
  7.2 18.3 %copy-start = (f32[32,2,8,512]{3,2,1,0:T(8,128)S(1)}, f32[32,2,8,512]{3,2,1,0:T(8,128)}, u32[]{:S(2)}) copy-start(f32[32,2,8,512]{3,2,1,0:T(8,128)} %param.4) | copy-start | bytes 3145732
  7.2 908.0 %all-reduce.6.cloned.1.call-start = ((), (), s32[]{:S(2)}) async-start(), calls=%async_computation | async-start | bytes 2097152 | tf_op jit(solution)/shard_map/psum | solution.py:67
  9.1 16.2 %collective-permute-start = (f32[32,2,8,512]{3,0,2,1:T(8,128)S(1)}, f32[32,2,8,512]{3,0,2,1:T(8,128)S(1)}, u32[]{:S(2)}, u32[]{:S(2)}) collective-permute-start(f32[32,2,8,512]{3,0,2,1:T(8,128)S(1)} %copy.36), channel_id=1, source_target_pairs={{0,16},{16,32},{32,48},{48,64},{64,80},{80,96},{96,112},{112,128},... | collective-permute-start | bytes 3145736 | tf_op jit(solution)/shard_map/ppermute | solution.py:19
  13.7 16.4 %collective-permute-start.1 = (f32[32,2,8,512]{3,0,2,1:T(8,128)S(1)}, f32[32,2,8,512]{3,0,2,1:T(8,128)S(1)}, u32[]{:S(2)}, u32[]{:S(2)}) collective-permute-start(f32[32,2,8,512]{3,0,2,1:T(8,128)S(1)} %copy.36), channel_id=1, source_target_pairs={{16,0},{32,16},{48,32},{64,48},{80,64},{96,80},{112,96},{128,112},... | collective-permute-start | bytes 3145736 | tf_op jit(solution)/shard_map/ppermute | solution.py:20
  30.2 40.8 %copy-start.3 = (f32[2,8,512]{2,1,0:T(8,128)S(1)}, f32[2,8,512]{2,1,0:T(8,128)}, u32[]{:S(2)}) copy-start(f32[2,8,512]{2,1,0:T(8,128)} %param.5) | copy-start | bytes 98308
  30.3 12.5 %collective-permute-start.2 = (f32[32,6,2,512]{3,0,2,1:T(8,128)S(1)}, f32[32,6,2,512]{3,0,2,1:T(8,128)S(1)}, u32[]{:S(2)}, u32[]{:S(2)}) collective-permute-start(f32[32,6,2,512]{3,0,2,1:T(8,128)S(1)} %get-tuple-element.23), channel_id=1, source_target_pairs={{0,1},{1,2},{2,3},{3,4},{4,5},{5,6},{6,7},{7,8},{8,9},{9,10},{10,1... | collective-permute-start | bytes 2359304 | tf_op jit(solution)/shard_map/ppermute | solution.py:19
  33.9 37.1 %collective-permute-start.3 = (f32[32,6,2,512]{3,0,2,1:T(8,128)S(1)}, f32[32,6,2,512]{3,0,2,1:T(8,128)S(1)}, u32[]{:S(2)}, u32[]{:S(2)}) collective-permute-start(f32[32,6,2,512]{3,0,2,1:T(8,128)S(1)} %get-tuple-element.24), channel_id=1, source_target_pairs={{1,0},{2,1},{3,2},{4,3},{5,4},{6,5},{7,6},{8,7},{9,8},{10,9},{11,1... | collective-permute-start | bytes 2359304 | tf_op jit(solution)/shard_map/ppermute | solution.py:20
  72.6 14.4 %collective-permute-start.4 = (f32[32,2,8,512]{3,0,2,1:T(8,128)S(1)}, f32[32,2,8,512]{3,0,2,1:T(8,128)S(1)}, u32[]{:S(2)}, u32[]{:S(2)}) collective-permute-start(f32[32,2,8,512]{3,0,2,1:T(8,128)S(1)} %get-tuple-element.15), channel_id=1, source_target_pairs={{0,16},{16,32},{32,48},{48,64},{64,80},{80,96},{96,112},{112,128},... | collective-permute-start | bytes 3145736 | tf_op jit(solution)/shard_map/ppermute | solution.py:19
  75.3 16.1 %collective-permute-start.5 = (f32[32,2,8,512]{3,0,2,1:T(8,128)S(1)}, f32[32,2,8,512]{3,0,2,1:T(8,128)S(1)}, u32[]{:S(2)}, u32[]{:S(2)}) collective-permute-start(f32[32,2,8,512]{3,0,2,1:T(8,128)S(1)} %get-tuple-element.15), channel_id=1, source_target_pairs={{16,0},{32,16},{48,32},{64,48},{80,64},{96,80},{112,96},{128,112},... | collective-permute-start | bytes 3145736 | tf_op jit(solution)/shard_map/ppermute | solution.py:20
  91.6 16.7 %collective-permute-start.6 = (f32[32,6,2,512]{3,0,2,1:T(8,128)S(1)}, f32[32,6,2,512]{3,0,2,1:T(8,128)S(1)}, u32[]{:S(2)}, u32[]{:S(2)}) collective-permute-start(f32[32,6,2,512]{3,0,2,1:T(8,128)S(1)} %get-tuple-element.21), channel_id=1, source_target_pairs={{0,1},{1,2},{2,3},{3,4},{4,5},{5,6},{6,7},{7,8},{8,9},{9,10},{10,1... | collective-permute-start | bytes 2359304 | tf_op jit(solution)/shard_map/ppermute | solution.py:19
  99.4 35.2 %collective-permute-start.7 = (f32[32,6,2,512]{3,0,2,1:T(8,128)S(1)}, f32[32,6,2,512]{3,0,2,1:T(8,128)S(1)}, u32[]{:S(2)}, u32[]{:S(2)}) collective-permute-start(f32[32,6,2,512]{3,0,2,1:T(8,128)S(1)} %get-tuple-element.22), channel_id=1, source_target_pairs={{1,0},{2,1},{3,2},{4,3},{5,4},{6,5},{7,6},{8,7},{9,8},{10,9},{11,1... | collective-permute-start | bytes 2359304 | tf_op jit(solution)/shard_map/ppermute | solution.py:20
  136.9 13.7 %collective-permute-start.8 = (f32[32,2,8,512]{3,0,2,1:T(8,128)S(1)}, f32[32,2,8,512]{3,0,2,1:T(8,128)S(1)}, u32[]{:S(2)}, u32[]{:S(2)}) collective-permute-start(f32[32,2,8,512]{3,0,2,1:T(8,128)S(1)} %fusion.21), channel_id=1, source_target_pairs={{0,16},{16,32},{32,48},{48,64},{64,80},{80,96},{96,112},{112,128},... | collective-permute-start | bytes 3145736 | tf_op jit(solution)/shard_map/ppermute | solution.py:19
  138.9 16.1 %collective-permute-start.9 = (f32[32,2,8,512]{3,0,2,1:T(8,128)S(1)}, f32[32,2,8,512]{3,0,2,1:T(8,128)S(1)}, u32[]{:S(2)}, u32[]{:S(2)}) collective-permute-start(f32[32,2,8,512]{3,0,2,1:T(8,128)S(1)} %fusion.21), channel_id=1, source_target_pairs={{16,0},{32,16},{48,32},{64,48},{80,64},{96,80},{112,96},{128,112},... | collective-permute-start | bytes 3145736 | tf_op jit(solution)/shard_map/ppermute | solution.py:20
  155.1 11.9 %collective-permute-start.10 = (f32[32,6,2,512]{3,0,2,1:T(8,128)S(1)}, f32[32,6,2,512]{3,0,2,1:T(8,128)S(1)}, u32[]{:S(2)}, u32[]{:S(2)}) collective-permute-start(f32[32,6,2,512]{3,0,2,1:T(8,128)S(1)} %get-tuple-element.19), channel_id=1, source_target_pairs={{0,1},{1,2},{2,3},{3,4},{4,5},{5,6},{6,7},{7,8},{8,9},{9,10},{10,1... | collective-permute-start | bytes 2359304 | tf_op jit(solution)/shard_map/ppermute | solution.py:19
  158.1 39.4 %copy-start.5 = (s32[2,8,512]{2,1,0:T(8,128)S(1)}, s32[2,8,512]{2,1,0:T(8,128)}, u32[]{:S(2)}) copy-start(s32[2,8,512]{2,1,0:T(8,128)} %param.6) | copy-start | bytes 98308
  158.2 39.5 %slice-start = ((s32[1,1,8192]{2,1,0:T(1,128)}), s32[1,1,4096]{2,1,0:T(1,128)S(1)}, s32[]{:S(2)}) async-start(s32[1,1,8192]{2,1,0:T(1,128)} %param.7), calls=%async_computation.1 | async-start | bytes 32768 | tf_op jit(solution)/shard_map/slice | solution.py:63
  158.2 33.2 %collective-permute-start.11 = (f32[32,6,2,512]{3,0,2,1:T(8,128)S(1)}, f32[32,6,2,512]{3,0,2,1:T(8,128)S(1)}, u32[]{:S(2)}, u32[]{:S(2)}) collective-permute-start(f32[32,6,2,512]{3,0,2,1:T(8,128)S(1)} %get-tuple-element.20), channel_id=1, source_target_pairs={{1,0},{2,1},{3,2},{4,3},{5,4},{6,5},{7,6},{8,7},{9,8},{10,9},{11,1... | collective-permute-start | bytes 2359304 | tf_op jit(solution)/shard_map/ppermute | solution.py:20
  193.2 13.7 %collective-permute-start.12 = (f32[32,2,8,512]{3,0,2,1:T(8,128)S(1)}, f32[32,2,8,512]{3,0,2,1:T(8,128)S(1)}, u32[]{:S(2)}, u32[]{:S(2)}) collective-permute-start(f32[32,2,8,512]{3,0,2,1:T(8,128)S(1)} %fusion.32), channel_id=1, source_target_pairs={{0,16},{16,32},{32,48},{48,64},{64,80},{80,96},{96,112},{112,128},... | collective-permute-start | bytes 3145736 | tf_op jit(solution)/shard_map/ppermute | solution.py:19
  195.1 33.7 %collective-permute-start.13 = (f32[32,2,8,512]{3,0,2,1:T(8,128)S(1)}, f32[32,2,8,512]{3,0,2,1:T(8,128)S(1)}, u32[]{:S(2)}, u32[]{:S(2)}) collective-permute-start(f32[32,2,8,512]{3,0,2,1:T(8,128)S(1)} %fusion.32), channel_id=1, source_target_pairs={{16,0},{32,16},{48,32},{64,48},{80,64},{96,80},{112,96},{128,112},... | collective-permute-start | bytes 3145736 | tf_op jit(solution)/shard_map/ppermute | solution.py:20
  197.7 37.3 %copy-start.4 = (s32[1,1,8192]{2,1,0:T(1,128)S(1)}, s32[1,1,8192]{2,1,0:T(1,128)}, u32[]{:S(2)}) copy-start(s32[1,1,8192]{2,1,0:T(1,128)} %param.7) | copy-start | bytes 98308
  206.8 23.4 %copy-start.1 = (f32[32,2,8,512]{3,0,2,1:T(8,128)}, f32[32,2,8,512]{3,0,2,1:T(8,128)S(1)}, u32[]{:S(2)}) copy-start(f32[32,2,8,512]{3,0,2,1:T(8,128)S(1)} %collective-permute-done.12) | copy-start | bytes 3145732
  228.8 1.5 copy-start.2
  230.3 11.8 %collective-permute-start.14 = (f32[32,6,2,512]{3,0,2,1:T(8,128)}, f32[32,6,2,512]{3,0,2,1:T(8,128)}, u32[]{:S(2)}, u32[]{:S(2)}) collective-permute-start(f32[32,6,2,512]{3,0,2,1:T(8,128)} %get-tuple-element.17), channel_id=1, source_target_pairs={{0,1},{1,2},{2,3},{3,4},{4,5},{5,6},{6,7},{7,8},{8,9},{9,10},{10,1... | collective-permute-start | bytes 2359304 | tf_op jit(solution)/shard_map/ppermute | solution.py:19
  233.7 36.1 %collective-permute-start.15 = (f32[32,6,2,512]{3,0,2,1:T(8,128)}, f32[32,6,2,512]{3,0,2,1:T(8,128)}, u32[]{:S(2)}, u32[]{:S(2)}) collective-permute-start(f32[32,6,2,512]{3,0,2,1:T(8,128)} %get-tuple-element.18), channel_id=1, source_target_pairs={{1,0},{2,1},{3,2},{4,3},{5,4},{6,5},{7,6},{8,7},{9,8},{10,9},{11,1... | collective-permute-start | bytes 2359304 | tf_op jit(solution)/shard_map/ppermute | solution.py:20
Sparse Core Ops, SparseCore 0:
  299.9 615.2 all-reduce.5
where the time goes:
time: 939 us; the launch traced here: 938 us
  waiting for transfers between devices  819 us (87%)
  starting transfers between devices  46.6 us (5%)
  local copies, waits for them, and re-layouts  27.6 us (3%)
  other arithmetic  20.5 us (2%)
  between operations  14.5 us (2%)
  matrix products  9.67 us (1%)
    psum x1, waiting for transfers between devices, shards(): total = lax.psum(term, ('gx', 'gy'))  615 us
    ppermute x8, waiting for transfers between devices, padded_2(): after = lax.ppermute(initial, axis, down)  141 us
    ppermute x8, waiting for transfers between devices, padded_2(): before = lax.ppermute(last, axis, up)  63.2 us
    ppermute x8, starting transfers between devices, padded_2(): before = lax.ppermute(last, axis, up)  28.9 us
  transfers between devices with their start and end apart: 17, of which 17 were waited for; matrix products, arithmetic and copies ran while one was open for 0% of the time, Pallas kernels for 0%

commit v1 on v0

--- a/solution.py
+++ b/solution.py
@@ -2,6 +2,7 @@
 import jax.numpy as jnp
 from jax import lax
 from jax.sharding import PartitionSpec as P
+from jax.lax import psum
 
 M = 4096
 HIGHEST = lax.Precision.HIGHEST
@@ -64,7 +65,8 @@
     devices = lax.axis_size("gx") * lax.axis_size("gy")
     term = (picked / jnp.sqrt(jnp.float32(M * devices))).reshape(2, count, M)
     width = M // devices
-    total = lax.psum(term, ("gx", "gy"))
+    prepare_flows_on = lambda array_here: psum(psum(array_here, axis_name="gy"), axis_name="gx")
+    total = prepare_flows_on(term)
     position = lax.axis_index("gx") * lax.axis_size("gy") + lax.axis_index("gy")
     share = lax.dynamic_slice_in_dim(total, position * width, width, 2)
     gram = jnp.dot(total[0], total[0].T, precision=HIGHEST) / cells

time: 939 us -> 1000 us (1.065)
  waiting for transfers between devices: 819 us -> 880 us
    psum x1 -> x2, waiting for transfers between devices: 615 us -> 676 us  [the longest x1 362 us: shards(): psum(psum(array_here, axis_name='gy'), axis_name='gx')]
  transfers between devices with their start and end apart: 17 -> 18, of which waited for: 17 -> 18; matrix products, arithmetic and copies ran while one was open for 0% -> 0% of each run, Pallas kernels for 0% -> 0%
where the time goes in v1:
time: 1000 us; the launch traced here: 999 us
  waiting for transfers between devices  880 us (88%)
  starting transfers between devices  47 us (5%)
  local copies, waits for them, and re-layouts  27.6 us (3%)
  other arithmetic  20.3 us (2%)
  between operations  14.5 us (1%)
    psum x1, waiting for transfers between devices, shards(): psum(psum(array_here, axis_name='gy'), axis_name='gx')  362 us
    psum x1, waiting for transfers between devices, shards(): psum(array_here, axis_name='gy')  313 us
    ppermute x8, waiting for transfers between devices, padded_2(): after = lax.ppermute(initial, axis, down)  141 us
    ppermute x8, waiting for transfers between devices, padded_2(): before = lax.ppermute(last, axis, up)  63 us
    ppermute x8, starting transfers between devices, padded_2(): before = lax.ppermute(last, axis, up)  28.9 us
  transfers between devices with their start and end apart: 18, of which 18 were waited for; matrix products, arithmetic and copies ran while one was open for 0% of the time, Pallas kernels for 0%

profile of v1, /device:TPU:1, one launch (start us, length us, event | category | flops | bytes accessed | tf_op | source)
XLA Modules:
  0.0 999.4 jit_solution(14002218086486717917)
XLA Ops:
  7.2 1.9 copy.36
  9.1 4.5 collective-permute-start
  13.7 5.6 collective-permute-start.1
  19.3 6.1 collective-permute-done
  25.5 0.6 constant_dynamic-update-slice_fusion.1
  26.1 4.0 collective-permute-done.1
  30.3 3.6 collective-permute-start.2
  33.9 1.3 collective-permute-start.3
  35.2 7.6 collective-permute-done.2
  42.8 28.2 %collective-permute-done.3 = f32[32,6,2,512]{3,0,2,1:T(8,128)S(1)} collective-permute-done((f32[32,6,2,512]{3,0,2,1:T(8,128)S(1)}, f32[32,6,2,512]{3,0,2,1:T(8,128)S(1)}, u32[]{:S(2)}, u32[]{:S(2)}) %collective-permute-start.3) | collective-permute-done | bytes 786464 | tf_op jit(solution)/shard_map/ppermute | solution.py:21
  71.0 1.6 broadcast_multiply_fusion
  72.6 2.7 collective-permute-start.4
  75.3 1.9 collective-permute-start.5
  77.3 9.8 collective-permute-done.4
  87.1 4.4 collective-permute-done.5
  91.6 7.8 collective-permute-start.6
  99.4 1.3 collective-permute-start.7
  100.7 7.6 collective-permute-done.6
  108.2 26.3 %collective-permute-done.7 = f32[32,6,2,512]{3,0,2,1:T(8,128)S(1)} collective-permute-done((f32[32,6,2,512]{3,0,2,1:T(8,128)S(1)}, f32[32,6,2,512]{3,0,2,1:T(8,128)S(1)}, u32[]{:S(2)}, u32[]{:S(2)}) %collective-permute-start.7) | collective-permute-done | bytes 786464 | tf_op jit(solution)/shard_map/ppermute | solution.py:21
  134.6 2.4 fusion.21
  136.9 1.9 collective-permute-start.8
  138.9 2.5 collective-permute-start.9
  141.3 9.2 collective-permute-done.8
  150.6 4.4 collective-permute-done.9
  155.1 3.0 collective-permute-start.10
  158.2 1.3 collective-permute-start.11
  159.5 7.5 collective-permute-done.10
  167.0 24.4 %collective-permute-done.11 = f32[32,6,2,512]{3,0,2,1:T(8,128)S(1)} collective-permute-done((f32[32,6,2,512]{3,0,2,1:T(8,128)S(1)}, f32[32,6,2,512]{3,0,2,1:T(8,128)S(1)}, u32[]{:S(2)}, u32[]{:S(2)}) %collective-permute-start.11) | collective-permute-done | bytes 786464 | tf_op jit(solution)/shard_map/ppermute | solution.py:21
  191.4 1.8 fusion.32
  193.2 1.9 collective-permute-start.12
  195.1 2.5 collective-permute-start.13
  197.7 9.1 collective-permute-done.12
  206.8 22.0 %collective-permute-done.13 = f32[32,2,8,512]{3,0,2,1:T(8,128)S(1)} collective-permute-done((f32[32,2,8,512]{3,0,2,1:T(8,128)S(1)}, f32[32,2,8,512]{3,0,2,1:T(8,128)S(1)}, u32[]{:S(2)}, u32[]{:S(2)}) %collective-permute-start.13) | collective-permute-done | bytes 1048608 | tf_op jit(solution)/shard_map/ppermute | solution.py:21
  228.8 1.5 pad_maximum_fusion.30
  230.3 3.5 collective-permute-start.14
  233.7 1.5 collective-permute-start.15
  235.2 0.6 copy.46
  235.9 6.1 collective-permute-done.14
  242.1 27.8 %collective-permute-done.15 = f32[32,6,2,512]{3,0,2,1:T(8,128)} collective-permute-done((f32[32,6,2,512]{3,0,2,1:T(8,128)}, f32[32,6,2,512]{3,0,2,1:T(8,128)}, u32[]{:S(2)}, u32[]{:S(2)}) %collective-permute-start.15) | collective-permute-done | bytes 786464 | tf_op jit(solution)/shard_map/ppermute | solution.py:21
  269.9 3.2 fusion.40
  273.0 1.6 copy.47
  274.6 1.3 concatenate.101
  275.9 2.0 fusion
  277.9 2.1 convolution_bitcast_fusion
  280.0 2.7 copy.57
  282.8 13.0 %gather_fusion = f32[4096,64]{1,0:T(8,128)S(1)} fusion(f32[64,8192]{0,1:T(8,128)} %bitcast.60, s32[4096]{0:T(1024)S(1)} %broadcast_clamp_fusion), kind=kCustom, calls=%fused_computation | custom fusion | bytes 2113536 | tf_op jit(solution)/shard_map/jit(_take)/gather | solution.py:64
  295.7 1.6 copy.49
  297.3 2.3 select_multiply_fusion
  299.6 0.3 all-reduce.9.cloned.1.call-start
  299.9 313.4 %all-reduce.7.cloned.1.call-done = f32[2,32,4096]{2,1,0:T(8,128)} async-done(((f32[2,32,4096]{2,1,0:T(8,128)}), f32[2,32,4096]{2,1,0:T(8,128)}) %all-reduce.7.cloned.1.call-update) | async-done | bytes 1048592 | tf_op jit(solution)/shard_map/psum | solution.py:68
  613.3 0.6 copy.59
  613.9 362.4 %all-reduce.9.cloned.1.call-done = f32[2,32,4096]{2,1,0:T(8,128)} async-done(((f32[2,32,4096]{2,1,0:T(8,128)}), f32[2,32,4096]{2,1,0:T(8,128)}) %all-reduce.9.cloned.1.call-update) | async-done | bytes 1048592 | tf_op jit(solution)/shard_map/psum | solution.py:68
  976.4 1.8 fusion.81
  978.2 2.9 cholesky.17
  981.2 0.6 compare_reduce_fusion
  981.8 0.7 fusion.117
  982.5 2.4 custom-call.6
  984.9 0.2 fusion.120
  985.1 1.8 convolution_multiply_fusion
  987.3 0.6 fusion.119
  987.9 1.6 fusion.78
  989.5 1.6 copy.54
  991.1 0.8 constant_dynamic-slice_fusion
  991.9 0.7 copy.55
  (42 shorter events, 1.3 us)
Async XLA Ops:
  7.2 18.3 %copy-start = (f32[32,2,8,512]{3,2,1,0:T(8,128)S(1)}, f32[32,2,8,512]{3,2,1,0:T(8,128)}, u32[]{:S(2)}) copy-start(f32[32,2,8,512]{3,2,1,0:T(8,128)} %param.4) | copy-start | bytes 3145732
  7.2 606.1 %all-reduce.7.cloned.1.call-start = ((), (), s32[]{:S(2)}) async-start(), calls=%async_computation | async-start | bytes 2097152 | tf_op jit(solution)/shard_map/psum | solution.py:68
  9.1 16.2 %collective-permute-start = (f32[32,2,8,512]{3,0,2,1:T(8,128)S(1)}, f32[32,2,8,512]{3,0,2,1:T(8,128)S(1)}, u32[]{:S(2)}, u32[]{:S(2)}) collective-permute-start(f32[32,2,8,512]{3,0,2,1:T(8,128)S(1)} %copy.36), channel_id=1, source_target_pairs={{0,16},{16,32},{32,48},{48,64},{64,80},{80,96},{96,112},{112,128},... | collective-permute-start | bytes 3145736 | tf_op jit(solution)/shard_map/ppermute | solution.py:20
  13.7 16.4 %collective-permute-start.1 = (f32[32,2,8,512]{3,0,2,1:T(8,128)S(1)}, f32[32,2,8,512]{3,0,2,1:T(8,128)S(1)}, u32[]{:S(2)}, u32[]{:S(2)}) collective-permute-start(f32[32,2,8,512]{3,0,2,1:T(8,128)S(1)} %copy.36), channel_id=1, source_target_pairs={{16,0},{32,16},{48,32},{64,48},{80,64},{96,80},{112,96},{128,112},... | collective-permute-start | bytes 3145736 | tf_op jit(solution)/shard_map/ppermute | solution.py:21
  30.2 40.8 %copy-start.3 = (f32[2,8,512]{2,1,0:T(8,128)S(1)}, f32[2,8,512]{2,1,0:T(8,128)}, u32[]{:S(2)}) copy-start(f32[2,8,512]{2,1,0:T(8,128)} %param.5) | copy-start | bytes 98308
  30.3 12.5 %collective-permute-start.2 = (f32[32,6,2,512]{3,0,2,1:T(8,128)S(1)}, f32[32,6,2,512]{3,0,2,1:T(8,128)S(1)}, u32[]{:S(2)}, u32[]{:S(2)}) collective-permute-start(f32[32,6,2,512]{3,0,2,1:T(8,128)S(1)} %get-tuple-element.23), channel_id=1, source_target_pairs={{0,1},{1,2},{2,3},{3,4},{4,5},{5,6},{6,7},{7,8},{8,9},{9,10},{10,1... | collective-permute-start | bytes 2359304 | tf_op jit(solution)/shard_map/ppermute | solution.py:20
  33.9 37.1 %collective-permute-start.3 = (f32[32,6,2,512]{3,0,2,1:T(8,128)S(1)}, f32[32,6,2,512]{3,0,2,1:T(8,128)S(1)}, u32[]{:S(2)}, u32[]{:S(2)}) collective-permute-start(f32[32,6,2,512]{3,0,2,1:T(8,128)S(1)} %get-tuple-element.24), channel_id=1, source_target_pairs={{1,0},{2,1},{3,2},{4,3},{5,4},{6,5},{7,6},{8,7},{9,8},{10,9},{11,1... | collective-permute-start | bytes 2359304 | tf_op jit(solution)/shard_map/ppermute | solution.py:21
  72.6 14.4 %collective-permute-start.4 = (f32[32,2,8,512]{3,0,2,1:T(8,128)S(1)}, f32[32,2,8,512]{3,0,2,1:T(8,128)S(1)}, u32[]{:S(2)}, u32[]{:S(2)}) collective-permute-start(f32[32,2,8,512]{3,0,2,1:T(8,128)S(1)} %get-tuple-element.15), channel_id=1, source_target_pairs={{0,16},{16,32},{32,48},{48,64},{64,80},{80,96},{96,112},{112,128},... | collective-permute-start | bytes 3145736 | tf_op jit(solution)/shard_map/ppermute | solution.py:20
  75.3 16.1 %collective-permute-start.5 = (f32[32,2,8,512]{3,0,2,1:T(8,128)S(1)}, f32[32,2,8,512]{3,0,2,1:T(8,128)S(1)}, u32[]{:S(2)}, u32[]{:S(2)}) collective-permute-start(f32[32,2,8,512]{3,0,2,1:T(8,128)S(1)} %get-tuple-element.15), channel_id=1, source_target_pairs={{16,0},{32,16},{48,32},{64,48},{80,64},{96,80},{112,96},{128,112},... | collective-permute-start | bytes 3145736 | tf_op jit(solution)/shard_map/ppermute | solution.py:21
  91.6 16.7 %collective-permute-start.6 = (f32[32,6,2,512]{3,0,2,1:T(8,128)S(1)}, f32[32,6,2,512]{3,0,2,1:T(8,128)S(1)}, u32[]{:S(2)}, u32[]{:S(2)}) collective-permute-start(f32[32,6,2,512]{3,0,2,1:T(8,128)S(1)} %get-tuple-element.21), channel_id=1, source_target_pairs={{0,1},{1,2},{2,3},{3,4},{4,5},{5,6},{6,7},{7,8},{8,9},{9,10},{10,1... | collective-permute-start | bytes 2359304 | tf_op jit(solution)/shard_map/ppermute | solution.py:20
  99.4 35.2 %collective-permute-start.7 = (f32[32,6,2,512]{3,0,2,1:T(8,128)S(1)}, f32[32,6,2,512]{3,0,2,1:T(8,128)S(1)}, u32[]{:S(2)}, u32[]{:S(2)}) collective-permute-start(f32[32,6,2,512]{3,0,2,1:T(8,128)S(1)} %get-tuple-element.22), channel_id=1, source_target_pairs={{1,0},{2,1},{3,2},{4,3},{5,4},{6,5},{7,6},{8,7},{9,8},{10,9},{11,1... | collective-permute-start | bytes 2359304 | tf_op jit(solution)/shard_map/ppermute | solution.py:21
  136.9 13.7 %collective-permute-start.8 = (f32[32,2,8,512]{3,0,2,1:T(8,128)S(1)}, f32[32,2,8,512]{3,0,2,1:T(8,128)S(1)}, u32[]{:S(2)}, u32[]{:S(2)}) collective-permute-start(f32[32,2,8,512]{3,0,2,1:T(8,128)S(1)} %fusion.21), channel_id=1, source_target_pairs={{0,16},{16,32},{32,48},{48,64},{64,80},{80,96},{96,112},{112,128},... | collective-permute-start | bytes 3145736 | tf_op jit(solution)/shard_map/ppermute | solution.py:20
  138.9 16.1 %collective-permute-start.9 = (f32[32,2,8,512]{3,0,2,1:T(8,128)S(1)}, f32[32,2,8,512]{3,0,2,1:T(8,128)S(1)}, u32[]{:S(2)}, u32[]{:S(2)}) collective-permute-start(f32[32,2,8,512]{3,0,2,1:T(8,128)S(1)} %fusion.21), channel_id=1, source_target_pairs={{16,0},{32,16},{48,32},{64,48},{80,64},{96,80},{112,96},{128,112},... | collective-permute-start | bytes 3145736 | tf_op jit(solution)/shard_map/ppermute | solution.py:21
  155.1 11.9 %collective-permute-start.10 = (f32[32,6,2,512]{3,0,2,1:T(8,128)S(1)}, f32[32,6,2,512]{3,0,2,1:T(8,128)S(1)}, u32[]{:S(2)}, u32[]{:S(2)}) collective-permute-start(f32[32,6,2,512]{3,0,2,1:T(8,128)S(1)} %get-tuple-element.19), channel_id=1, source_target_pairs={{0,1},{1,2},{2,3},{3,4},{4,5},{5,6},{6,7},{7,8},{8,9},{9,10},{10,1... | collective-permute-start | bytes 2359304 | tf_op jit(solution)/shard_map/ppermute | solution.py:20
  158.1 39.4 %copy-start.5 = (s32[2,8,512]{2,1,0:T(8,128)S(1)}, s32[2,8,512]{2,1,0:T(8,128)}, u32[]{:S(2)}) copy-start(s32[2,8,512]{2,1,0:T(8,128)} %param.6) | copy-start | bytes 98308
  158.2 39.5 %slice-start = ((s32[1,1,8192]{2,1,0:T(1,128)}), s32[1,1,4096]{2,1,0:T(1,128)S(1)}, s32[]{:S(2)}) async-start(s32[1,1,8192]{2,1,0:T(1,128)} %param.7), calls=%async_computation.2 | async-start | bytes 32768 | tf_op jit(solution)/shard_map/slice | solution.py:64
  158.2 33.2 %collective-permute-start.11 = (f32[32,6,2,512]{3,0,2,1:T(8,128)S(1)}, f32[32,6,2,512]{3,0,2,1:T(8,128)S(1)}, u32[]{:S(2)}, u32[]{:S(2)}) collective-permute-start(f32[32,6,2,512]{3,0,2,1:T(8,128)S(1)} %get-tuple-element.20), channel_id=1, source_target_pairs={{1,0},{2,1},{3,2},{4,3},{5,4},{6,5},{7,6},{8,7},{9,8},{10,9},{11,1... | collective-permute-start | bytes 2359304 | tf_op jit(solution)/shard_map/ppermute | solution.py:21
  193.2 13.7 %collective-permute-start.12 = (f32[32,2,8,512]{3,0,2,1:T(8,128)S(1)}, f32[32,2,8,512]{3,0,2,1:T(8,128)S(1)}, u32[]{:S(2)}, u32[]{:S(2)}) collective-permute-start(f32[32,2,8,512]{3,0,2,1:T(8,128)S(1)} %fusion.32), channel_id=1, source_target_pairs={{0,16},{16,32},{32,48},{48,64},{64,80},{80,96},{96,112},{112,128},... | collective-permute-start | bytes 3145736 | tf_op jit(solution)/shard_map/ppermute | solution.py:20
  195.1 33.7 %collective-permute-start.13 = (f32[32,2,8,512]{3,0,2,1:T(8,128)S(1)}, f32[32,2,8,512]{3,0,2,1:T(8,128)S(1)}, u32[]{:S(2)}, u32[]{:S(2)}) collective-permute-start(f32[32,2,8,512]{3,0,2,1:T(8,128)S(1)} %fusion.32), channel_id=1, source_target_pairs={{16,0},{32,16},{48,32},{64,48},{80,64},{96,80},{112,96},{128,112},... | collective-permute-start | bytes 3145736 | tf_op jit(solution)/shard_map/ppermute | solution.py:21
  197.7 37.5 %copy-start.4 = (s32[1,1,8192]{2,1,0:T(1,128)S(1)}, s32[1,1,8192]{2,1,0:T(1,128)}, u32[]{:S(2)}) copy-start(s32[1,1,8192]{2,1,0:T(1,128)} %param.7) | copy-start | bytes 98308
  206.8 23.4 %copy-start.1 = (f32[32,2,8,512]{3,0,2,1:T(8,128)}, f32[32,2,8,512]{3,0,2,1:T(8,128)S(1)}, u32[]{:S(2)}) copy-start(f32[32,2,8,512]{3,0,2,1:T(8,128)S(1)} %collective-permute-done.12) | copy-start | bytes 3145732
  228.8 1.5 copy-start.2
  230.3 11.8 %collective-permute-start.14 = (f32[32,6,2,512]{3,0,2,1:T(8,128)}, f32[32,6,2,512]{3,0,2,1:T(8,128)}, u32[]{:S(2)}, u32[]{:S(2)}) collective-permute-start(f32[32,6,2,512]{3,0,2,1:T(8,128)} %get-tuple-element.17), channel_id=1, source_target_pairs={{0,1},{1,2},{2,3},{3,4},{4,5},{5,6},{6,7},{7,8},{8,9},{9,10},{10,1... | collective-permute-start | bytes 2359304 | tf_op jit(solution)/shard_map/ppermute | solution.py:20
  233.7 36.1 %collective-permute-start.15 = (f32[32,6,2,512]{3,0,2,1:T(8,128)}, f32[32,6,2,512]{3,0,2,1:T(8,128)}, u32[]{:S(2)}, u32[]{:S(2)}) collective-permute-start(f32[32,6,2,512]{3,0,2,1:T(8,128)} %get-tuple-element.18), channel_id=1, source_target_pairs={{1,0},{2,1},{3,2},{4,3},{5,4},{6,5},{7,6},{8,7},{9,8},{10,9},{11,1... | collective-permute-start | bytes 2359304 | tf_op jit(solution)/shard_map/ppermute | solution.py:21
  299.6 676.8 %all-reduce.9.cloned.1.call-start = ((), (), s32[]{:S(2)}) async-start(), calls=%async_computation.1 | async-start | bytes 2097152 | tf_op jit(solution)/shard_map/psum | solution.py:68
Sparse Core Ops, SparseCore 0:
  299.7 313.4 all-reduce.6
  616.4 359.8 all-reduce.8
